TPU v7x, 256 devices: a whole 4x4x8 slice. The times are simulated.
256 devices in a mesh: dp: 32 (over x, z), mp: 8 (over y, core).
Axes of the slice: x: 4, y: 4, z: 8, core: 2. Of those that a mesh axis runs over, the one named last changes fastest.
Arguments:
- tokens: bfloat16 [8192, 8192], P(('dp', 'mp')), may hold values from -6 to 6
- upstream: bfloat16 [8192, 2, 28672], P(('dp', 'mp')), may hold values from -0.0625 to 0.0625
- deltas: bfloat16 [1024, 128, 128], P('mp'), may hold values from -0.5 to 0.5
- block_row: int32 [1024], P('mp'), may hold values from 0 to 63, as said below
- block_column: int32 [1024], P('mp'), may hold values from 0 to 55, as said below
- block_owner: int32 [1024], P('mp'), may hold values from 0 to 31, as said below
- block_count: int32 [8], P('mp'), may hold values from 64 to 128, as said below
Outputs:
- branch_out: bfloat16 [8192, 2, 28672], P('dp', None, 'mp')
- block_grads: float32 [8, 192, 128, 128], P('mp', 'dp')
Inputs may be any that keep to these rules, and one draw needn't show every extreme that they name: `block_row`: row tile of each slot's delta tile. `block_column`: column tile within the shard's gate columns (below 28) followed by its up columns; the tiles of one shard's slots are distinct. `block_owner`: among the live slots of one shard no dp index owns more than 6 tiles, and in every shard one dp index owns exactly 6. The live slots of a shard are its first block_count slots; some shard has all 128 live.
All inputs are finite; a program needn't handle non-finite values.
Results may differ from a plain program's by a relative error of at most 0.001.
Values may be sent and summed in bfloat16 or wider, within the bound.
No kernel may reach another device: no remote copies, remote signals or barrier semaphores. Data moves between devices by JAX's collectives and lax.ppermute only.
A program may use at most 128 MiB of HBM per device.

v0:
```python
import jax
import jax.numpy as jnp
from jax import lax
from jax.sharding import PartitionSpec as P


def pick_tiles(source, chosen):
    slot_ids = jnp.arange(chosen.shape[1], dtype=jnp.int32)
    source_index = jnp.sum(jnp.where(chosen, slot_ids[None, :], 0), axis=1)
    present = jnp.any(chosen, axis=1).astype(jnp.float32)
    return jnp.take(source, source_index, axis=0) * present[:, None, None]


def local(tokens, upstream, deltas, block_row, block_column, block_owner, block_count):
    model_width = tokens.shape[1]
    tile_size = deltas.shape[1]
    slot_count = deltas.shape[0]
    hidden = lax.all_to_all(upstream, "mp", split_axis=2, concat_axis=0, tiled=True)
    group_rows = hidden.shape[0]
    column_blocks = hidden.shape[1] * hidden.shape[2] // tile_size
    hidden_major = jnp.transpose(hidden.reshape(group_rows, column_blocks, tile_size), (1, 0, 2))
    upstream_chosen = jnp.take(hidden_major, block_column, axis=0)
    slot_ids = jnp.arange(slot_count, dtype=jnp.int32)
    live_slots = slot_ids < block_count[0]
    column_table = (
        live_slots[:, None]
        & (block_column[:, None] == jnp.arange(column_blocks, dtype=jnp.int32)[None, :])
    ).astype(jnp.float32)
    shard_rows = lax.all_gather(tokens, "mp", axis=0, tiled=True)
    row_count = shard_rows.shape[0]
    row_major = jnp.transpose(
        shard_rows.reshape(row_count, model_width // tile_size, tile_size), (1, 0, 2)
    )
    feature_tiles = jnp.take(row_major, block_row, axis=0)
    product = jnp.einsum("kni,kio->kno", feature_tiles, deltas, preferred_element_type=jnp.float32)
    rows_out = jnp.einsum("kc,kno->cno", column_table, product, precision=lax.Precision.HIGHEST)
    placed = rows_out
    grad_sum = jnp.einsum(
        "kni,kno->kio", feature_tiles, upstream_chosen, preferred_element_type=jnp.float32
    )
    placed, grad_sum = (placed, grad_sum)
    branch_out = jnp.transpose(placed.astype(jnp.bfloat16), (1, 0, 2)).reshape(
        group_rows, hidden.shape[1], hidden.shape[2]
    )
    dp_count = lax.axis_size("dp")
    owner_cap = 3 * slot_count // (2 * dp_count)
    owner_hot = (
        (block_owner[:, None] == jnp.arange(dp_count, dtype=jnp.int32)[None, :])
        & live_slots[:, None]
    ).astype(jnp.int32)
    before = jnp.cumsum(owner_hot, axis=0) - owner_hot
    owner_rank = jnp.sum(before * owner_hot, axis=1)
    summed = lax.psum(grad_sum, "dp")
    my_owner = lax.axis_index("dp")
    chosen = (
        live_slots[None, :]
        & (block_owner[None, :] == my_owner)
        & (owner_rank[None, :] == jnp.arange(owner_cap, dtype=jnp.int32)[:, None])
    )
    owned = pick_tiles(summed, chosen)
    return (branch_out, owned[None])


def solution(mesh):
    placed = (
        P(("dp", "mp"), None),
        P(("dp", "mp"), None, None),
        P("mp", None, None),
        P("mp"),
        P("mp"),
        P("mp"),
        P("mp"),
    )
    return jax.shard_map(
        local,
        mesh=mesh,
        in_specs=placed,
        out_specs=(P("dp", None, "mp"), P("mp", "dp", None, None)),
        check_vma=False,
    )
```

profile of v0, /device:TPU:1, one launch (start us, length us, event | category | flops | bytes accessed | tf_op | source)
XLA Modules:
  0.0 435.7 jit_solution(1149873122995598057)
XLA Ops:
  7.2 0.0 all-gather.2.cloned.1.call-start
  7.2 0.7 all-gather.2.cloned.1.call-update
  7.9 34.9 %copy.36 = bf16[32,2,28672]{0,1,2:T(2,128)(2,1)} copy(bf16[32,2,28672]{2,1,0:T(2,128)(2,1)} %param.8) | data formatting | bytes 7340032 | tf_op args[1]
  42.8 0.0 copy-start.2
  42.8 0.0 copy-start.1
  42.8 16.5 %reshape.95 = bf16[8,2,114688]{2,1,0:T(2,128)(2,1)} reshape(bf16[28672,2,32]{2,1,0:T(2,128)(2,1)} %bitcast.26) | data formatting | bytes 7340032
  59.4 7.6 %all-to-all-start = ((bf16[8,2,114688]{2,1,0:T(2,128)(2,1)}), bf16[8,2,114688]{2,1,0:T(2,128)(2,1)}, u32[]{:S(2)}, u32[]{:S(2)}) async-start(bf16[8,2,114688]{2,1,0:T(2,128)(2,1)} %reshape.95), calls=%async_computation | async-start | bytes 7340032 | tf_op jit(solution)/shard_map/all_to_all | solution.py:18
  66.9 0.0 all-reduce.2.cloned.1.call-start
  66.9 0.0 copy-done.2
  67.0 0.0 copy-done.1
  67.0 43.1 %all-to-all-done = bf16[8,2,114688]{2,1,0:T(2,128)(2,1)} async-done(((bf16[8,2,114688]{2,1,0:T(2,128)(2,1)}), bf16[8,2,114688]{2,1,0:T(2,128)(2,1)}, u32[]{:S(2)}, u32[]{:S(2)}) %all-to-all-start) | async-done | bytes 3670048 | tf_op jit(solution)/shard_map/all_to_all | solution.py:18
  110.1 11.6 %reshape.96 = bf16[28672,2,32]{2,1,0:T(2,128)(2,1)} reshape(bf16[8,2,114688]{2,1,0:T(2,128)(2,1)} %all-to-all-done) | data formatting | bytes 7340032
  121.7 35.0 %copy.37 = bf16[32,2,8,3584]{3,1,0,2:T(2,128)(2,1)} copy(bf16[32,2,8,3584]{0,1,3,2:T(2,128)(2,1)} %bitcast.25) | data formatting | bytes 7340032 | tf_op jit(solution)/shard_map/all_to_all | solution.py:18
  156.8 9.2 %reshape.67 = bf16[256,56,128]{2,1,0:T(8,128)(2,1)} reshape(bf16[8,32,2,3584]{3,2,1,0:T(2,128)(2,1)} %bitcast.30) | data formatting | bytes 7340032 | tf_op jit(solution)/shard_map/reshape | solution.py:21
  165.9 4.8 %copy.46 = bf16[256,56,128]{2,0,1:T(8,128)(2,1)} copy(bf16[256,56,128]{2,1,0:T(8,128)(2,1)} %reshape.67) | data formatting | bytes 7340032 | tf_op jit(solution)/shard_map/reshape | solution.py:21
  170.7 8.6 %gather_fusion.1 = bf16[128,256,128]{2,1,0:T(8,128)(2,1)} fusion(bf16[56,256,128]{2,1,0:T(8,128)(2,1)} %bitcast.27, s32[1024]{0:T(1024)S(1)} %pad_clamp_fusion.1), kind=kCustom, calls=%fused_computation.1 | custom fusion | bytes 16777728 | tf_op jit(solution)/shard_map/jit(_take)/gather | solution.py:22
  179.3 0.0 all-gather.2.cloned.1.call-done
  179.3 6.4 %copy.33 = bf16[256,8192]{0,1:T(8,128)(2,1)} copy(bf16[256,8192]{1,0:T(8,128)(2,1)} %all-gather.2.cloned.1.call-done) | data formatting | bytes 8388608 | tf_op jit(solution)/shard_map/all_gather | solution.py:29
  185.7 6.4 %copy.34 = bf16[256,64,128]{2,0,1:T(8,128)(2,1)} copy(bf16[256,64,128]{0,2,1:T(8,128)(2,1)} %bitcast.29) | data formatting | bytes 8388608 | tf_op jit(solution)/shard_map/reshape | solution.py:32
  192.1 8.7 %gather_fusion = bf16[128,256,128]{2,1,0:T(8,128)(2,1)} fusion(bf16[64,256,128]{2,1,0:T(8,128)(2,1)} %bitcast.28, s32[1024]{0:T(1024)S(1)} %pad_clamp_fusion.2), kind=kCustom, calls=%fused_computation | custom fusion | bytes 16777728 | tf_op jit(solution)/shard_map/jit(_take)/gather | solution.py:34
  200.8 11.9 %fusion.2 = f32[128,128,128]{2,1,0:T(8,128)} fusion(bf16[128,256,128]{2,1,0:T(8,128)(2,1)} %gather_fusion.1, pred[128]{0:T(512)(128)(4,1)S(1)} %get-tuple-element.4, bf16[128,256,128]{2,1,0:T(8,128)(2,1)} %gather_fusion, pred[128]{0:T(512)(128)(4,1)S(1)} %get-tuple-element.5), kind=kOutput, calls=%fused_computation.5 | convolution fusion | flops 1082130432 | bytes 25166080 | tf_op jit(solution)/shard_map/kni,kno->kio/dot_general | solution.py:38
  212.7 0.0 copy-start
  212.7 0.0 all-reduce.2.cloned.1.call-update
  213.4 0.0 copy-done
  213.4 0.1 fusion.11
  213.5 0.2 reduce_window_sum.11
  213.7 0.2 select_reduce_fusion
  213.9 0.1 fusion.18
  214.0 0.1 select_reduce_fusion.1
  214.2 13.5 %fusion.6 = f32[128,256,128]{2,1,0:T(8,128)} fusion(bf16[128,128,128]{2,1,0:T(8,128)(2,1)} %param.9, bf16[128,256,128]{2,1,0:T(8,128)(2,1)} %gather_fusion, pred[128]{0:T(512)(128)(4,1)S(1)} %get-tuple-element.5), kind=kOutput, calls=%fused_computation.12 | convolution fusion | flops 1077936128 | bytes 29360256 | tf_op jit(solution)/shard_map/kni,kio->kno/dot_general | solution.py:35
  227.7 22.6 %convert_bitcast_fusion = bf16[256,56,128]{2,1,0:T(8,128)(2,1)} fusion(f32[128,256,128]{2,1,0:T(8,128)} %fusion.6, s32[128]{0:T(128)S(1)} %copy-done.1, pred[128]{0:T(512)(128)(4,1)S(1)} %get-tuple-element.3), kind=kOutput, calls=%fused_computation.11 | convolution fusion | flops 2820421632 | bytes 20447872 | tf_op jit(solution)/shard_map/kc,kno->cno/dot_general | solution.py:36
  250.4 8.2 %reshape.66 = bf16[256,2,3584]{2,1,0:T(2,128)(2,1)} reshape(bf16[256,56,128]{2,1,0:T(8,128)(2,1)} %convert_bitcast_fusion) | data formatting | bytes 7340032 | tf_op jit(solution)/shard_map/reshape | solution.py:42
  258.5 165.6 %all-reduce.2.cloned.1.call-done = f32[128,128,128]{2,1,0:T(8,128)} async-done(((f32[128,128,128]{2,1,0:T(8,128)}), f32[128,128,128]{2,1,0:T(8,128)}) %all-reduce.2.cloned.1.call-update) | async-done | bytes 8388624 | tf_op jit(solution)/shard_map/psum | solution.py:53
  424.1 4.0 gather_fusion.2
  428.0 0.9 fusion.9
  (10 shorter events, 0.1 us)
Async XLA Ops:
  7.2 172.2 %all-gather.2.cloned.1.call-start = ((), (), s32[]{:S(2)}) async-start(), calls=%async_computation.1 | async-start | bytes 4718592 | tf_op jit(solution)/shard_map/all_gather | solution.py:29
  42.8 24.1 %copy-start.2 = (s32[128]{0:T(128)S(1)}, s32[128]{0:T(128)}, u32[]{:S(2)}) copy-start(s32[128]{0:T(128)} %param.10) | copy-start | bytes 1540
  42.8 24.1 %copy-start.1 = (s32[128]{0:T(128)S(1)}, s32[128]{0:T(128)}, u32[]{:S(2)}) copy-start(s32[128]{0:T(128)} %param.11) | copy-start | bytes 1540
  59.4 50.7 %all-to-all-start = ((bf16[8,2,114688]{2,1,0:T(2,128)(2,1)}), bf16[8,2,114688]{2,1,0:T(2,128)(2,1)}, u32[]{:S(2)}, u32[]{:S(2)}) async-start(bf16[8,2,114688]{2,1,0:T(2,128)(2,1)} %reshape.95), calls=%async_computation | async-start | bytes 7340032 | tf_op jit(solution)/shard_map/all_to_all | solution.py:18
  66.9 357.1 %all-reduce.2.cloned.1.call-start = ((), (), s32[]{:S(2)}) async-start(), calls=%async_computation.2 | async-start | bytes 16777216 | tf_op jit(solution)/shard_map/psum | solution.py:53
  212.7 0.7 copy-start
Sparse Core Ops, SparseCore 0:
  9.8 38.8 all-gather.1
  212.9 211.1 all-reduce.1
where the time goes:
time: 440 us; the launch traced here: 436 us
  waiting for transfers between devices  209 us (48%)
  local copies, waits for them, and re-layouts  154 us (35%)
  matrix products  48.1 us (11%)
  between operations  14.8 us (3%)
  starting transfers between devices  7.59 us (2%)
    psum x1, waiting for transfers between devices, local(): summed = lax.psum(grad_sum, 'dp')  166 us
    unnamed x9, local copies, waits for them, and re-layouts  63.1 us
    all_to_all x1, waiting for transfers between devices, local(): lax.all_to_all(upstream, 'mp', split_axis=2, concat_axis=0, tiled=True)  43.1 us
    all_to_all x1, local copies, waits for them, and re-layouts, local(): lax.all_to_all(upstream, 'mp', split_axis=2, concat_axis=0, tiled=True)  35 us
    dot_general x1, matrix products, local(): jnp.einsum('kc,kno->cno', column_table, product, precision=lax.Precision....  22.6 us
    reshape x2, local copies, waits for them, and re-layouts, local(): hidden.reshape(group_rows, column_blocks, tile_size)  14 us
    dot_general x1, matrix products, local(): jnp.einsum('kni,kio->kno', feature_tiles, deltas, preferred_element_type=...  13.5 us
    dot_general x1, matrix products, local(): jnp.einsum('kni,kno->kio', feature_tiles, upstream_chosen, preferred_elem...  11.9 us
  transfers between devices with their start and end apart: 3, of which 2 were waited for; matrix products, arithmetic and copies ran while one was open for 38% of the time, Pallas kernels for 0%

commit v1 on v0

--- a/solution.py
+++ b/solution.py
@@ -50,7 +50,9 @@
     ).astype(jnp.int32)
     before = jnp.cumsum(owner_hot, axis=0) - owner_hot
     owner_rank = jnp.sum(before * owner_hot, axis=1)
-    summed = lax.psum(grad_sum, "dp")
+    summed = grad_sum
+    for hop in (1, 2, 4, 8, 16):
+        summed = summed + lax.ppermute(summed, "dp", [(dev, dev ^ hop) for dev in range(32)])
     my_owner = lax.axis_index("dp")
     chosen = (
         live_slots[None, :]

time: 440 us -> 1570 us (3.57)
  waiting for transfers between devices: 209 us -> 1260 us
  other arithmetic: 1.61 us -> 60 us
    ppermute x0 -> x5, waiting for transfers between devices: none -> 1220 us  [local(): lax.ppermute(summed, 'dp', [(dev, dev ^ hop) for dev in range(32)])]
    psum x1 -> x0, waiting for transfers between devices: 166 us -> none  [local(): summed = lax.psum(grad_sum, 'dp')]
    add x0 -> x5, other arithmetic: none -> 58.4 us  [local(): summed + lax.ppermute(summed, 'dp', [(dev, dev ^ hop) for dev in range(32)])]
  transfers between devices with their start and end apart: 3 -> 7, of which waited for: 2 -> 6; matrix products, arithmetic and copies ran while one was open for 38% -> 11% of each run, Pallas kernels for 0% -> 0%
where the time goes in v1:
time: 1570 us; the launch traced here: 1560 us
  waiting for transfers between devices  1260 us (80%)
  local copies, waits for them, and re-layouts  154 us (10%)
  other arithmetic  60 us (4%)
  matrix products  47.4 us (3%)
  starting transfers between devices  19.1 us (1%)
    ppermute x5, waiting for transfers between devices, local(): lax.ppermute(summed, 'dp', [(dev, dev ^ hop) for dev in range(32)])  1220 us
    unnamed x9, local copies, waits for them, and re-layouts  63 us
    add x5, other arithmetic, local(): summed + lax.ppermute(summed, 'dp', [(dev, dev ^ hop) for dev in range(32)])  58.4 us
    all_to_all x1, waiting for transfers between devices, local(): lax.all_to_all(upstream, 'mp', split_axis=2, concat_axis=0, tiled=True)  43 us
    all_to_all x1, local copies, waits for them, and re-layouts, local(): lax.all_to_all(upstream, 'mp', split_axis=2, concat_axis=0, tiled=True)  35 us
  transfers between devices with their start and end apart: 7, of which 6 were waited for; matrix products, arithmetic and copies ran while one was open for 11% of the time, Pallas kernels for 0%

profile of v1, /device:TPU:1, one launch (start us, length us, event | category | flops | bytes accessed | tf_op | source)
XLA Modules:
  0.0 1556.4 jit_solution(786171603042988487)
XLA Ops:
  7.2 0.0 all-gather.2.cloned.1.call-start
  7.2 0.7 all-gather.2.cloned.1.call-update
  7.9 34.9 %copy.36 = bf16[32,2,28672]{0,1,2:T(2,128)(2,1)} copy(bf16[32,2,28672]{2,1,0:T(2,128)(2,1)} %param.8) | data formatting | bytes 7340032 | tf_op args[1]
  42.8 0.0 copy-start.2
  42.8 0.0 copy-start.1
  42.8 16.5 %reshape.95 = bf16[8,2,114688]{2,1,0:T(2,128)(2,1)} reshape(bf16[28672,2,32]{2,1,0:T(2,128)(2,1)} %bitcast.26) | data formatting | bytes 7340032
  59.4 8.1 all-to-all-start
  67.5 0.0 copy-done.2
  67.5 0.0 copy-done.1
  67.5 43.0 %all-to-all-done = bf16[8,2,114688]{2,1,0:T(2,128)(2,1)} async-done(((bf16[8,2,114688]{2,1,0:T(2,128)(2,1)}), bf16[8,2,114688]{2,1,0:T(2,128)(2,1)}, u32[]{:S(2)}, u32[]{:S(2)}) %all-to-all-start) | async-done | bytes 3670048 | tf_op jit(solution)/shard_map/all_to_all | solution.py:18
  110.6 11.6 reshape.96
  122.2 35.0 %copy.37 = bf16[32,2,8,3584]{3,1,0,2:T(2,128)(2,1)} copy(bf16[32,2,8,3584]{0,1,3,2:T(2,128)(2,1)} %bitcast.25) | data formatting | bytes 7340032 | tf_op jit(solution)/shard_map/all_to_all | solution.py:18
  157.2 9.2 reshape.67
  166.4 4.8 copy.46
  171.1 8.6 gather_fusion.1
  179.7 0.0 all-gather.2.cloned.1.call-done
  179.7 6.4 copy.33
  186.1 6.4 copy.34
  192.5 8.8 gather_fusion
  201.2 11.9 fusion.2
  213.2 0.2 collective-permute-start
  213.4 181.3 %collective-permute-done = f32[128,128,128]{2,1,0:T(8,128)} collective-permute-done((f32[128,128,128]{2,1,0:T(8,128)}, f32[128,128,128]{2,1,0:T(8,128)}, u32[]{:S(2)}, u32[]{:S(2)}) %collective-permute-start) | collective-permute-done | bytes 8388640 | tf_op jit(solution)/shard_map/ppermute | solution.py:55
  394.7 11.7 add.51
  406.4 1.6 collective-permute-start.1
  408.0 361.4 %collective-permute-done.1 = f32[128,128,128]{2,1,0:T(8,128)} collective-permute-done((f32[128,128,128]{2,1,0:T(8,128)}, f32[128,128,128]{2,1,0:T(8,128)}, u32[]{:S(2)}, u32[]{:S(2)}) %collective-permute-start.1) | collective-permute-done | bytes 8388640 | tf_op jit(solution)/shard_map/ppermute | solution.py:55
  769.4 11.7 add.52
  781.1 5.1 collective-permute-start.2
  786.2 361.4 %collective-permute-done.2 = f32[128,128,128]{2,1,0:T(8,128)} collective-permute-done((f32[128,128,128]{2,1,0:T(8,128)}, f32[128,128,128]{2,1,0:T(8,128)}, u32[]{:S(2)}, u32[]{:S(2)}) %collective-permute-start.2) | collective-permute-done | bytes 8388640 | tf_op jit(solution)/shard_map/ppermute | solution.py:55
  1147.6 11.7 add.53
  1159.3 0.0 copy-start
  1159.3 1.2 collective-permute-start.3
  1160.5 179.4 %collective-permute-done.3 = f32[128,128,128]{2,1,0:T(8,128)} collective-permute-done((f32[128,128,128]{2,1,0:T(8,128)}, f32[128,128,128]{2,1,0:T(8,128)}, u32[]{:S(2)}, u32[]{:S(2)}) %collective-permute-start.3) | collective-permute-done | bytes 8388640 | tf_op jit(solution)/shard_map/ppermute | solution.py:55
  1339.9 11.7 add.54
  1351.6 2.8 collective-permute-start.4
  1355.1 0.0 copy-done
  1355.1 0.1 fusion.11
  1355.2 0.2 reduce_window_sum.11
  1355.4 0.2 select_reduce_fusion
  1355.6 0.1 fusion.18
  1355.7 0.1 select_reduce_fusion.1
  1355.9 12.7 fusion.6
  1368.6 22.8 %convert_bitcast_fusion = bf16[256,56,128]{2,1,0:T(8,128)(2,1)} fusion(f32[128,256,128]{2,1,0:T(8,128)} %fusion.6, s32[128]{0:T(128)S(1)} %copy-done.1, pred[128]{0:T(512)(128)(4,1)S(1)} %get-tuple-element.3), kind=kOutput, calls=%fused_computation.11 | convolution fusion | flops 2820421632 | bytes 20447872 | tf_op jit(solution)/shard_map/kc,kno->cno/dot_general | solution.py:36
  1391.3 8.1 reshape.66
  1399.5 133.4 %collective-permute-done.4 = f32[128,128,128]{2,1,0:T(8,128)} collective-permute-done((f32[128,128,128]{2,1,0:T(8,128)}, f32[128,128,128]{2,1,0:T(8,128)}, u32[]{:S(2)}, u32[]{:S(2)}) %collective-permute-start.4) | collective-permute-done | bytes 8388640 | tf_op jit(solution)/shard_map/ppermute | solution.py:55
  1532.9 11.7 add.55
  1544.5 4.0 gather_fusion.2
  1548.5 0.9 fusion.9
  (10 shorter events, 0.1 us)
Async XLA Ops:
  7.2 172.6 %all-gather.2.cloned.1.call-start = ((), (), s32[]{:S(2)}) async-start(), calls=%async_computation.1 | async-start | bytes 4718592 | tf_op jit(solution)/shard_map/all_gather | solution.py:29
  42.8 24.7 %copy-start.2 = (s32[128]{0:T(128)S(1)}, s32[128]{0:T(128)}, u32[]{:S(2)}) copy-start(s32[128]{0:T(128)} %param.10) | copy-start | bytes 1540
  42.8 24.7 %copy-start.1 = (s32[128]{0:T(128)S(1)}, s32[128]{0:T(128)}, u32[]{:S(2)}) copy-start(s32[128]{0:T(128)} %param.11) | copy-start | bytes 1540
  59.4 51.2 %all-to-all-start = ((bf16[8,2,114688]{2,1,0:T(2,128)(2,1)}), bf16[8,2,114688]{2,1,0:T(2,128)(2,1)}, u32[]{:S(2)}, u32[]{:S(2)}) async-start(bf16[8,2,114688]{2,1,0:T(2,128)(2,1)} %reshape.95), calls=%async_computation | async-start | bytes 7340032 | tf_op jit(solution)/shard_map/all_to_all | solution.py:18
  213.2 181.5 %collective-permute-start = (f32[128,128,128]{2,1,0:T(8,128)}, f32[128,128,128]{2,1,0:T(8,128)}, u32[]{:S(2)}, u32[]{:S(2)}) collective-permute-start(f32[128,128,128]{2,1,0:T(8,128)} %fusion.2), channel_id=1, source_target_pairs={{0,8},{8,0},{16,24},{24,16},{32,40},{40,32},{48,56},{56,48},{64,72... | collective-permute-start | bytes 25165832 | tf_op jit(solution)/shard_map/ppermute | solution.py:55
  406.4 363.0 %collective-permute-start.1 = (f32[128,128,128]{2,1,0:T(8,128)}, f32[128,128,128]{2,1,0:T(8,128)}, u32[]{:S(2)}, u32[]{:S(2)}) collective-permute-start(f32[128,128,128]{2,1,0:T(8,128)} %add.51), channel_id=1, source_target_pairs={{0,16},{8,24},{16,0},{24,8},{32,48},{40,56},{48,32},{56,40},{64,80... | collective-permute-start | bytes 25165832 | tf_op jit(solution)/shard_map/ppermute | solution.py:55
  781.1 366.6 %collective-permute-start.2 = (f32[128,128,128]{2,1,0:T(8,128)}, f32[128,128,128]{2,1,0:T(8,128)}, u32[]{:S(2)}, u32[]{:S(2)}) collective-permute-start(f32[128,128,128]{2,1,0:T(8,128)} %add.52), channel_id=1, source_target_pairs={{0,32},{8,40},{16,48},{24,56},{32,0},{40,8},{48,16},{56,24},{64,96... | collective-permute-start | bytes 25165832 | tf_op jit(solution)/shard_map/ppermute | solution.py:55
  1159.3 195.8 %copy-start = (s32[128]{0:T(128)S(1)}, s32[128]{0:T(128)}, u32[]{:S(2)}) copy-start(s32[128]{0:T(128)} %param.12) | copy-start | bytes 1540
  1159.3 180.6 %collective-permute-start.3 = (f32[128,128,128]{2,1,0:T(8,128)}, f32[128,128,128]{2,1,0:T(8,128)}, u32[]{:S(2)}, u32[]{:S(2)}) collective-permute-start(f32[128,128,128]{2,1,0:T(8,128)} %add.53), channel_id=1, source_target_pairs={{0,64},{8,72},{16,80},{24,88},{32,96},{40,104},{48,112},{56,120},{... | collective-permute-start | bytes 25165832 | tf_op jit(solution)/shard_map/ppermute | solution.py:55
  1351.6 181.2 %collective-permute-start.4 = (f32[128,128,128]{2,1,0:T(8,128)}, f32[128,128,128]{2,1,0:T(8,128)}, u32[]{:S(2)}, u32[]{:S(2)}) collective-permute-start(f32[128,128,128]{2,1,0:T(8,128)} %add.54), channel_id=1, source_target_pairs={{0,128},{8,136},{16,144},{24,152},{32,160},{40,168},{48,176},{56,1... | collective-permute-start | bytes 25165832 | tf_op jit(solution)/shard_map/ppermute | solution.py:55
Sparse Core Ops, SparseCore 0:
  9.8 38.8 all-gather.1
